TPU v7x, 256 devices: a whole 4x4x8 slice. The times are simulated.
256 devices in a mesh: cfg: 2 (over z_lo), req: 16 (over y, z_hi), mlp: 8 (over x, core).
Axes of the slice: x: 4, y: 4, z: 8 (z_hi: 4, z_lo: 2; z = z_hi * 2 + z_lo), core: 2. Of those that a mesh axis runs over, the one named last changes fastest.
Arguments:
- hidden: bfloat16 [2, 16384, 1152], P('cfg', ('req', 'mlp')), may hold values from -64 to 64
- noisy_latent: float32 [16384, 16], P(('req', 'mlp'), 'cfg'), may hold values from -6 to 6
- labels: int32 [16, 4], replicated, may hold values from 0 to 999
- timesteps: int32 [16, 4], replicated, may hold values from 0 to 999
- lengths: int32 [16, 4], P('req'), may hold values from 1 to 512, 1024 in all within a row
- guidance: float32 [16, 4], P('req'), may hold values from 1.5 to 4
- keep_scale: float32 [16, 4], P('req'), may hold values from 0.9 to 1.2
- noise_scale: float32 [16, 4], P('req'), may hold values from -0.8 to -0.2
- class_table: bfloat16 [1001, 1152], replicated, may hold values from -6 to 6
- time_up: bfloat16 [256, 1152], replicated, may hold values from -0.375 to 0.375
- time_up_bias: bfloat16 [1152], replicated, may hold values from -4 to 4
- time_out: bfloat16 [1152, 1152], replicated, may hold values from -0.1875 to 0.1875
- time_out_bias: bfloat16 [1152], replicated, may hold values from -4 to 4
- mod_weight: bfloat16 [1152, 9216], P(None, 'req'), may hold values from -0.1875 to 0.1875
- mod_bias: bfloat16 [9216], P('req'), may hold values from -4 to 4
- qkv_weight: bfloat16 [1152, 3456], P(None, 'req'), may hold values from -8 to 8
- qkv_bias: bfloat16 [3456], P('req'), may hold values from -4 to 4
- out_weight: bfloat16 [1152, 1152], P(None, 'req'), may hold values from -0.1875 to 0.1875
- out_bias: bfloat16 [1152], P('req'), may hold values from -4 to 4
- up_weight: bfloat16 [1152, 4608], P(None, 'mlp'), may hold values from -0.1875 to 0.1875
- up_bias: bfloat16 [4608], P('mlp'), may hold values from -4 to 4
- down_weight: bfloat16 [4608, 1152], P('mlp'), may hold values from -1 to 1
- down_bias: bfloat16 [1152], replicated, may hold values from -4 to 4
- final_weight: bfloat16 [1152, 16], replicated, may hold values from -0.1875 to 0.1875
- final_bias: bfloat16 [16], replicated, may hold values from -4 to 4
Outputs:
- next_latent: float32 [16384, 16], P(('req', 'mlp'), 'cfg')
Inputs may be any that keep to these rules, and one draw needn't show every extreme that they name: `lengths`: each row sums to 1024, and its largest crop has exactly 512 tokens.
All inputs are finite; a program needn't handle non-finite values.
Results may differ from a plain program's by a relative error of at most 0.015.
Values may be sent and summed in bfloat16 or wider, within the bound.
No kernel may reach another device: no remote copies, remote signals or barrier semaphores. Data moves between devices by JAX's collectives and lax.ppermute only.
A program may use at most 128 MiB of HBM per device.

v0:
```python
import math
import jax
import jax.numpy as jnp
from jax import lax
from jax.sharding import PartitionSpec as P

HEADS = 16
HEAD_DIM = 72
CLASSES = 1000
FREQ = 256


def layer_norm(values):
    values = values.astype(jnp.float32)
    centre = values - jnp.mean(values, axis=-1, keepdims=True)
    variance = jnp.mean(centre * centre, axis=-1, keepdims=True)
    return centre * lax.rsqrt(variance + 1e-06)


def time_features(times_flat):
    half_freq = FREQ // 2
    frequency = jnp.exp(-math.log(10000.0) * jnp.arange(half_freq, dtype=jnp.float32) / half_freq)
    angles = times_flat.astype(jnp.float32)[:, None] * frequency[None, :]
    return jnp.concatenate([jnp.cos(angles), jnp.sin(angles)], axis=1).astype(jnp.bfloat16)


def segment_ids(lengths_row, positions):
    ends = jnp.cumsum(lengths_row)
    return jnp.sum((positions[:, None] >= ends[None, :]).astype(jnp.int32), axis=1)


def attention(queries, keys_all, values_all, query_segment, key_segment):
    scores = jnp.einsum(
        "qhd,khd->hqk", queries, keys_all, preferred_element_type=jnp.float32
    ) / math.sqrt(HEAD_DIM)
    same = (query_segment[:, None] == key_segment[None, :])[None]
    masked = jnp.where(same, scores, -1e30)
    row_max = jnp.max(masked, axis=2, keepdims=True)
    expo = jnp.where(same, jnp.exp(masked - row_max), 0.0)
    denominator = jnp.sum(expo, axis=2)
    weights = expo.astype(jnp.bfloat16)
    mixed = jnp.einsum("hqk,khd->qhd", weights, values_all, preferred_element_type=jnp.float32)
    result = mixed / jnp.transpose(denominator)[:, :, None]
    return result.astype(jnp.bfloat16).reshape(queries.shape[0], -1)


def shards(
    hidden,
    noisy_latent,
    labels,
    timesteps,
    lengths,
    guidance,
    keep_scale,
    noise_scale,
    class_table,
    time_up,
    time_up_bias,
    time_out,
    time_out_bias,
    mod_weight,
    mod_bias,
    qkv_weight,
    qkv_bias,
    out_weight,
    out_bias,
    up_weight,
    up_bias,
    down_weight,
    down_bias,
    final_weight,
    final_bias,
):
    req_count = lax.axis_size("req")
    mlp_count = lax.axis_size("mlp")
    half_index = lax.axis_index("cfg")
    mlp_index = lax.axis_index("mlp")
    tok_rows = hidden.shape[1]
    width = hidden.shape[2]
    group_rows = tok_rows * mlp_count
    per_group = labels.shape[1]
    time_feat = time_features(timesteps.reshape(-1))
    time_mid = jax.nn.silu(
        jnp.dot(time_feat, time_up, preferred_element_type=jnp.float32)
        + time_up_bias.astype(jnp.float32)
    ).astype(jnp.bfloat16)
    time_cond = jnp.dot(
        time_mid, time_out, preferred_element_type=jnp.float32
    ) + time_out_bias.astype(jnp.float32)
    used_labels = jnp.where(half_index == 0, labels.reshape(-1), CLASSES)
    one_hot = (used_labels[:, None] == jnp.arange(CLASSES + 1, dtype=jnp.int32)[None, :]).astype(
        jnp.bfloat16
    )
    cond_act = jax.nn.silu(
        time_cond + jnp.dot(one_hot, class_table, preferred_element_type=jnp.float32)
    ).astype(jnp.bfloat16)
    local_mod = (
        jnp.dot(cond_act, mod_weight, preferred_element_type=jnp.float32)
        + mod_bias.astype(jnp.float32)
    ).astype(jnp.bfloat16)
    local_mod = local_mod.reshape(req_count, per_group, local_mod.shape[1])
    modulation = lax.all_to_all(local_mod, "req", split_axis=0, concat_axis=2, tiled=True)[0]
    positions = jnp.arange(group_rows, dtype=jnp.int32)
    segment_all = segment_ids(lengths[0], positions)
    segment_own = lax.dynamic_slice_in_dim(segment_all, mlp_index * tok_rows, tok_rows)
    member = segment_own[:, None] == jnp.arange(per_group, dtype=jnp.int32)[None, :]
    per_token = jnp.dot(member.astype(jnp.bfloat16), modulation, preferred_element_type=jnp.float32)
    pieces = [per_token[:, index * width : (index + 1) * width] for index in range(8)]
    shift_attn, scale_attn, gate_attn, shift_mlp, scale_mlp, gate_mlp, shift_final, scale_final = (
        pieces
    )
    rows = hidden[0]
    normed = (layer_norm(rows) * (1.0 + scale_attn) + shift_attn).astype(jnp.bfloat16)
    qkv_full, qkv_bias_full, out_full, out_bias_full = (
        lax.all_gather(qkv_weight, "req", axis=1, tiled=True),
        lax.all_gather(qkv_bias, "req", axis=0, tiled=True),
        lax.all_gather(out_weight, "req", axis=1, tiled=True),
        lax.all_gather(out_bias, "req", axis=0, tiled=True),
    )
    qkv = (
        jnp.dot(normed, qkv_full, preferred_element_type=jnp.float32)
        + qkv_bias_full.astype(jnp.float32)
    ).astype(jnp.bfloat16)
    keys_all, values_all = (
        lax.all_gather(qkv[:, width : 2 * width], "mlp", axis=0, tiled=True),
        lax.all_gather(qkv[:, 2 * width :], "mlp", axis=0, tiled=True),
    )
    attended = attention(
        qkv[:, :width].reshape(tok_rows, HEADS, HEAD_DIM),
        keys_all.reshape(group_rows, HEADS, HEAD_DIM),
        values_all.reshape(group_rows, HEADS, HEAD_DIM),
        segment_own,
        segment_all,
    )
    projected = jnp.dot(
        attended, out_full, preferred_element_type=jnp.float32
    ) + out_bias_full.astype(jnp.float32)
    mid_hidden = (rows.astype(jnp.float32) + gate_attn * projected).astype(jnp.bfloat16)
    normed_mlp = (layer_norm(mid_hidden) * (1.0 + scale_mlp) + shift_mlp).astype(jnp.bfloat16)
    gathered = lax.all_gather(normed_mlp, "mlp", axis=0, tiled=True)
    inner = jax.nn.gelu(
        jnp.dot(gathered, up_weight, preferred_element_type=jnp.float32)
        + up_bias.astype(jnp.float32),
        approximate=True,
    ).astype(jnp.bfloat16)
    mlp_out = lax.psum_scatter(
        jnp.dot(inner, down_weight, preferred_element_type=jnp.float32).astype(jnp.bfloat16),
        "mlp",
        scatter_dimension=0,
        tiled=True,
    ).astype(jnp.float32)
    final_hidden = mid_hidden.astype(jnp.float32) + gate_mlp * (
        mlp_out + down_bias.astype(jnp.float32)
    )
    normed_final = (layer_norm(final_hidden) * (1.0 + scale_final) + shift_final).astype(
        jnp.bfloat16
    )
    predicted = jnp.dot(
        normed_final, final_weight, preferred_element_type=jnp.float32
    ) + final_bias.astype(jnp.float32)
    halves = lax.all_to_all(predicted[None], "cfg", split_axis=2, concat_axis=0, tiled=True)
    eps_cond = halves[0]
    eps_free = halves[1]
    member_f = member.astype(jnp.float32)
    guide_tok = jnp.sum(member_f * guidance, axis=1, keepdims=True)
    keep_tok = jnp.sum(member_f * keep_scale, axis=1, keepdims=True)
    noise_tok = jnp.sum(member_f * noise_scale, axis=1, keepdims=True)
    return keep_tok * noisy_latent + noise_tok * (eps_free + guide_tok * (eps_cond - eps_free))


def solution(mesh):
    return jax.shard_map(
        shards,
        mesh=mesh,
        in_specs=(
            P("cfg", ("req", "mlp"), None),
            P(("req", "mlp"), "cfg"),
            P(),
            P(),
            P("req", None),
            P("req", None),
            P("req", None),
            P("req", None),
            P(),
            P(),
            P(),
            P(),
            P(),
            P(None, "req"),
            P("req"),
            P(None, "req"),
            P("req"),
            P(None, "req"),
            P("req"),
            P(None, "mlp"),
            P("mlp"),
            P("mlp", None),
            P(),
            P(),
            P(),
        ),
        out_specs=P(("req", "mlp"), "cfg"),
        check_vma=False,
    )
```

profile of v0, /device:TPU:8, one launch (start us, length us, event | category | flops | bytes accessed | tf_op | source)
XLA Modules:
  0.0 357.1 jit_solution(16776291229437060213)
XLA Ops:
  6.5 0.7 all-gather.6.cloned.1.call-update
  7.3 0.8 convert_element_type.94
  8.2 0.7 convert_element_type.96
  8.9 0.7 convert_element_type.98
  9.6 0.7 broadcast_select_fusion
  10.4 0.7 convert_element_type.100
  11.4 1.8 convolution_add_fusion.3
  13.2 3.0 fusion.29
  16.2 0.7 reshape.143
  16.9 11.6 %all-to-all-start = ((bf16[16,4,576]{2,1,0:T(4,128)(2,1)}), bf16[16,4,576]{2,1,0:T(4,128)(2,1)S(1)}, u32[]{:S(2)}, u32[]{:S(2)}) async-start(bf16[16,4,576]{2,1,0:T(4,128)(2,1)} %reshape.143), calls=%async_computation | async-start | bytes 163840 | tf_op jit(solution)/shard_map/all_to_all | solution.py:102
  31.1 82.8 %all-reduce.2 = (bf16[3456]{0:T(1024)(128)(2,1)S(1)}, bf16[1152]{0:T(1024)(128)(2,1)S(1)}) all-reduce(bf16[3456]{0:T(1024)(128)(2,1)S(1)} %dynamic-update-slice, bf16[1152]{0:T(1024)(128)(2,1)S(1)} %dynamic-update-slice.1), channel_id=1, replica_groups=mesh['cfg'=2,'req'=16,'mlp'=8] {'req'}, use_global_device_ids=true, to_apply=%add | all-reduce | flops 4608 | bytes 18432
  114.6 3.0 fusion.67
  117.6 6.1 %fusion.2 = bf16[128,3456]{1,0:T(8,128)(2,1)S(1)} fusion(bf16[1152,3456]{0,1:T(8,128)(2,1)} %all-gather.6.cloned.1.call-done, f32[3456]{0:T(1024)S(1)} %convert_element_type.103, bf16[1,128,1152]{2,1,0:T(8,128)(2,1)S(1)} %copy-done.1, f32[128,9216]{1,0:T(8,128)} %fusion.67, f32[128]{0:T(128)S(1)} %add_rsqrt_fusion.2, f32[128]{0:T(128)S(1)} %broadcast_multiply_fusion.2), kind=kOutput, calls=%fused_computation.5 | convolution fusion | flops 1021132800 | bytes 10336768 | tf_op jit(solution)/shard_map/dot_general | solution.py:121
  123.7 0.9 fusion.83
  124.7 0.7 all-gather.8.cloned.1.call-update
  126.2 0.8 broadcast_compare_fusion
  127.2 37.7 %all-gather.10.cloned.1.call-done = bf16[1024,1152]{1,0:T(8,128)(2,1)} async-done(((bf16[128,1152]{1,0:T(8,128)(2,1)}), bf16[1024,1152]{1,0:T(8,128)(2,1)}) %all-gather.10.cloned.1.call-update) | async-done | bytes 2359312 | tf_op jit(solution)/shard_map/all_gather | solution.py:125
  164.9 4.3 %copy.52 = bf16[1024,1152]{0,1:T(8,128)(2,1)} copy(bf16[1024,1152]{1,0:T(8,128)(2,1)} %all-gather.10.cloned.1.call-done) | data formatting | bytes 4718592 | tf_op jit(solution)/shard_map/all_gather | solution.py:125
  169.2 26.3 %all-gather.8.cloned.1.call-done = bf16[1024,1152]{1,0:T(8,128)(2,1)} async-done(((bf16[128,1152]{1,0:T(8,128)(2,1)}), bf16[1024,1152]{1,0:T(8,128)(2,1)}) %all-gather.8.cloned.1.call-update) | async-done | bytes 2359312 | tf_op jit(solution)/shard_map/all_gather | solution.py:126
  195.5 4.3 %copy.50 = bf16[1024,1152]{0,1:T(8,128)(2,1)} copy(bf16[1024,1152]{1,0:T(8,128)(2,1)} %all-gather.8.cloned.1.call-done) | data formatting | bytes 4718592 | tf_op jit(solution)/shard_map/all_gather | solution.py:126
  199.8 7.5 %fusion.84 = (f32[16,128]{1,0:T(8,128)S(1)}, bf16[16,128,1024]{2,1,0:T(8,128)(2,1)}) fusion(pred[128,1024]{1,0:T(8,128)(4,1)S(1)} %copy-done.2, bf16[128,16,72]{0,2,1:T(8,128)(2,1)S(1)} %bitcast.88, bf16[1024,16,72]{0,2,1:T(8,128)(2,1)} %bitcast.84), kind=kOutput, calls=%fused_computation.112 | convolution fusion | flops 314573824 | bytes 6987776 | tf_op jit(solution)/shard_map/sub | solution.py:39
  207.2 5.2 %fusion.26 = bf16[128,16,72]{0,2,1:T(8,128)(2,1)} fusion(bf16[1024,16,72]{0,2,1:T(8,128)(2,1)} %bitcast.85, bf16[16,128,1024]{2,1,0:T(8,128)(2,1)} %get-tuple-element.18, f32[128,16]{0,1:T(8,128)S(1)} %bitcast.95), kind=kOutput, calls=%fused_computation.31 | convolution fusion | flops 302284800 | bytes 6856704 | tf_op jit(solution)/shard_map/hqk,khd->qhd/dot_general | solution.py:42
  212.4 49.4 %all-gather.12.cloned.1.call-done = bf16[1152,1152]{0,1:T(8,128)(2,1)} async-done(((bf16[1152,72]{0,1:T(8,128)(2,1)}), bf16[1152,1152]{0,1:T(8,128)(2,1)}) %all-gather.12.cloned.1.call-update) | async-done | bytes 2654224 | tf_op jit(solution)/shard_map/all_gather | solution.py:117
  261.8 3.0 fusion.85
  265.0 2.2 fusion.41
  267.3 26.1 %all-gather.14.cloned.1.call-done = bf16[1024,1152]{1,0:T(8,128)(2,1)} async-done(((bf16[128,1152]{1,0:T(8,128)(2,1)}), bf16[1024,1152]{1,0:T(8,128)(2,1)}) %all-gather.14.cloned.1.call-update) | async-done | bytes 2359312 | tf_op jit(solution)/shard_map/all_gather | solution.py:140
  293.4 7.8 %convolution_convert_fusion = bf16[1024,1152]{1,0:T(8,128)(2,1)} fusion(bf16[576,1152]{1,0:T(8,128)(2,1)} %param.46, bf16[1024,1152]{1,0:T(8,128)(2,1)} %all-gather.14.cloned.1.call-done, bf16[1152,576]{0,1:T(8,128)(2,1)} %param.44, f32[576]{0:T(1024)S(1)} %convert_element_type.111), kind=kOutput, calls=%fused_computation.11 | convolution fusion | flops 2724986880 | bytes 7375104 | tf_op jit(solution)/shard_map/dot_general | solution.py:147
  301.9 36.9 %reduce-scatter.2.cloned.1.call-done = bf16[128,1152]{1,0:T(8,128)(2,1)} async-done(((bf16[1024,1152]{1,0:T(8,128)(2,1)}), bf16[128,1152]{1,0:T(8,128)(2,1)}) %reduce-scatter.2.cloned.1.call-update) | async-done | bytes 294928 | tf_op jit(solution)/shard_map/reduce_scatter | solution.py:146
  338.8 1.3 fusion.81
  340.4 2.2 convolution_add_fusion.6
  342.6 3.2 all-to-all-start.1
  345.9 3.7 %all-to-all-done.1 = f32[1,128,16]{1,0,2:T(1,128)S(1)} async-done(((f32[1,128,16]{1,0,2:T(1,128)}), f32[1,128,16]{1,0,2:T(1,128)S(1)}, u32[]{:S(2)}, u32[]{:S(2)}) %all-to-all-start.1) | async-done | bytes 8224 | tf_op jit(solution)/shard_map/all_to_all | solution.py:161
  (76 shorter events, 5.5 us)
Async XLA Ops:
  6.5 4.8 %copy-start = (bf16[1152,1152]{1,0:T(8,128)(2,1)S(1)}, bf16[1152,1152]{1,0:T(8,128)(2,1)}, u32[]{:S(2)}) copy-start(bf16[1152,1152]{1,0:T(8,128)(2,1)} %param.36) | copy-start | bytes 7962628
  6.5 111.0 %all-gather.6.cloned.1.call-start = ((), (), s32[]{:S(2)}) async-start(), calls=%async_computation.3 | async-start | bytes 8460288 | tf_op jit(solution)/shard_map/all_gather | solution.py:115
  13.2 15.4 %copy-start.10 = (s32[1,4]{1,0:T(1,128)S(1)}, s32[1,4]{1,0:T(1,128)}, u32[]{:S(2)}) copy-start(s32[1,4]{1,0:T(1,128)} %param.29) | copy-start | bytes 52
  13.2 15.5 %copy-start.14 = (u32[256]{0:T(256)S(1)}, u32[256]{0:T(256)}, u32[]{:S(2)}) copy-start(u32[256]{0:T(256)} %constant.70) | copy-start | bytes 3076
  13.2 17.4 %copy-start.11 = (bf16[216]{0:T(256)(128)(2,1)S(1)}, bf16[216]{0:T(256)(128)(2,1)}, u32[]{:S(2)}) copy-start(bf16[216]{0:T(256)(128)(2,1)} %param.41) | copy-start | bytes 1300
  13.2 17.7 %copy-start.12 = (bf16[72]{0:T(256)(128)(2,1)S(1)}, bf16[72]{0:T(256)(128)(2,1)}, u32[]{:S(2)}) copy-start(bf16[72]{0:T(256)(128)(2,1)} %param.43) | copy-start | bytes 436
  13.2 100.9 %copy-start.1 = (bf16[1,128,1152]{2,1,0:T(8,128)(2,1)S(1)}, bf16[1,128,1152]{2,1,0:T(8,128)(2,1)}, u32[]{:S(2)}) copy-start(bf16[1,128,1152]{2,1,0:T(8,128)(2,1)} %param.25) | copy-start | bytes 884740
  16.9 97.5 %all-to-all-start = ((bf16[16,4,576]{2,1,0:T(4,128)(2,1)}), bf16[16,4,576]{2,1,0:T(4,128)(2,1)S(1)}, u32[]{:S(2)}, u32[]{:S(2)}) async-start(bf16[16,4,576]{2,1,0:T(4,128)(2,1)} %reshape.143), calls=%async_computation | async-start | bytes 163840 | tf_op jit(solution)/shard_map/all_to_all | solution.py:102
  28.5 136.4 %all-gather.10.cloned.1.call-start = ((), (), s32[]{:S(2)}) async-start(), calls=%async_computation.5 | async-start | bytes 2654208 | tf_op jit(solution)/shard_map/all_gather | solution.py:125
  124.6 70.8 %all-gather.8.cloned.1.call-start = ((), (), s32[]{:S(2)}) async-start(), calls=%async_computation.4 | async-start | bytes 2654208 | tf_op jit(solution)/shard_map/all_gather | solution.py:126
  125.4 136.4 %all-gather.12.cloned.1.call-start = ((), (), s32[]{:S(2)}) async-start(), calls=%async_computation.6 | async-start | bytes 2820096 | tf_op jit(solution)/shard_map/all_gather | solution.py:117
  125.9 167.4 %all-gather.14.cloned.1.call-start = ((), (), s32[]{:S(2)}) async-start(), calls=%async_computation.7 | async-start | bytes 2654208 | tf_op jit(solution)/shard_map/all_gather | solution.py:140
  169.2 30.6 %copy-start.2 = (pred[128,1024]{1,0:T(8,128)(4,1)S(1)}, pred[128,1024]{1,0:T(8,128)(4,1)}, u32[]{:S(2)}) copy-start(pred[128,1024]{1,0:T(8,128)(4,1)} %broadcast_compare_fusion) | copy-start | bytes 393220
  264.8 2.5 copy-start.6
  267.2 71.7 %reduce-scatter.2.cloned.1.call-start = ((), (), s32[]{:S(2)}) async-start(), calls=%async_computation.8 | async-start | bytes 2654208 | tf_op jit(solution)/shard_map/reduce_scatter | solution.py:146
  301.2 0.7 copy-start.4
  301.2 0.7 copy-start.13
  301.2 39.2 %copy-start.3 = (bf16[1152,16]{0,1:T(8,128)(2,1)S(1)}, bf16[1152,16]{0,1:T(8,128)(2,1)}, u32[]{:S(2)}) copy-start(bf16[1152,16]{0,1:T(8,128)(2,1)} %param.48) | copy-start | bytes 110596
  301.9 43.9 %copy-start.7 = (f32[1,4]{1,0:T(1,128)S(1)}, f32[1,4]{1,0:T(1,128)}, u32[]{:S(2)}) copy-start(f32[1,4]{1,0:T(1,128)} %param.31) | copy-start | bytes 52
  301.9 44.0 %copy-start.8 = (f32[1,4]{1,0:T(1,128)S(1)}, f32[1,4]{1,0:T(1,128)}, u32[]{:S(2)}) copy-start(f32[1,4]{1,0:T(1,128)} %param.30) | copy-start | bytes 52
  301.9 44.0 %copy-start.9 = (f32[1,4]{1,0:T(1,128)S(1)}, f32[1,4]{1,0:T(1,128)}, u32[]{:S(2)}) copy-start(f32[1,4]{1,0:T(1,128)} %param.32) | copy-start | bytes 52
  301.9 47.7 %copy-start.5 = (f32[128,8]{0,1:T(8,128)S(1)}, f32[128,8]{0,1:T(8,128)}, u32[]{:S(2)}) copy-start(f32[128,8]{0,1:T(8,128)} %param.26) | copy-start | bytes 12292
  342.6 7.0 %all-to-all-start.1 = ((f32[1,128,16]{1,0,2:T(1,128)}), f32[1,128,16]{1,0,2:T(1,128)S(1)}, u32[]{:S(2)}, u32[]{:S(2)}) async-start(f32[1,128,16]{1,0,2:T(1,128)} %bitcast.16), calls=%async_computation.2 | async-start | bytes 16384 | tf_op jit(solution)/shard_map/all_to_all | solution.py:161
Sparse Core Ops, SparseCore 0:
  9.8 107.0 all-gather.5
  124.8 40.0 all-gather.9
  166.7 28.6 all-gather.7
  197.8 63.9 all-gather.11
  267.3 26.0 all-gather.13
  301.3 37.4 reduce-scatter.1
where the time goes:
time: 358 us; the launch traced here: 357 us
  waiting for transfers between devices  182 us (51%)
  blocking collectives  82.8 us (23%)
  matrix products  39.5 us (11%)
  starting transfers between devices  15.2 us (4%)
  between operations  15 us (4%)
  local copies, waits for them, and re-layouts  12.7 us (4%)
  other arithmetic  9.78 us (3%)
    unnamed x1, blocking collectives  82.8 us
    all_gather x1, waiting for transfers between devices, shards(): lax.all_gather(out_weight, 'req', axis=1, tiled=True)  49.4 us
    all_gather x1, waiting for transfers between devices, shards(): lax.all_gather(qkv[:, width:2 * width], 'mlp', axis=0, tiled=True)  37.7 us
    reduce_scatter x1, waiting for transfers between devices, shards(): lax.psum_scatter(jnp.dot(inner, down_weight, preferred_element_type=jnp.f...  36.9 us
    all_gather x1, waiting for transfers between devices, shards(): lax.all_gather(qkv[:, 2 * width:], 'mlp', axis=0, tiled=True)  26.3 us
    all_gather x1, waiting for transfers between devices, shards(): gathered = lax.all_gather(normed_mlp, 'mlp', axis=0, tiled=True)  26.1 us
    all_to_all x1, starting transfers between devices, shards(): lax.all_to_all(local_mod, 'req', split_axis=0, concat_axis=2, tiled=True)[0]  11.6 us
    dot_general x1, matrix products, shards(): jnp.dot(inner, down_weight, preferred_element_type=jnp.float32)  7.81 us
  transfers between devices with their start and end apart: 8, of which 6 were waited for; matrix products, arithmetic and copies ran while one was open for 10% of the time, Pallas kernels for 0%

commit v1 on v0

--- a/solution.py
+++ b/solution.py
@@ -8,6 +8,13 @@
 HEAD_DIM = 72
 CLASSES = 1000
 FREQ = 256
+
+
+def exchange_gather(x, name, d):
+    n_dev = lax.axis_size(name)
+    shards = jnp.stack([x for _ in range(n_dev)])
+    shards = lax.all_to_all(shards, name, split_axis=0, concat_axis=0)
+    return jnp.concatenate(shards, axis=d)
 
 
 def layer_norm(values):
@@ -114,7 +121,7 @@
     qkv_full, qkv_bias_full, out_full, out_bias_full = (
         lax.all_gather(qkv_weight, "req", axis=1, tiled=True),
         lax.all_gather(qkv_bias, "req", axis=0, tiled=True),
-        lax.all_gather(out_weight, "req", axis=1, tiled=True),
+        exchange_gather(out_weight, "req", 1),
         lax.all_gather(out_bias, "req", axis=0, tiled=True),
     )
     qkv = (

time: 358 us -> 311 us (0.87)
  waiting for transfers between devices: 182 us -> 115 us
  starting transfers between devices: 15.2 us -> 33.7 us
    all_gather x1 -> x0, waiting for transfers between devices: 49.4 us -> none  [shards(): lax.all_gather(out_weight, 'req', axis=1, tiled=True)]
    all_gather x1, waiting for transfers between devices: 37.7 us -> 18 us  [shards(): lax.all_gather(qkv[:, width:2 * width], 'mlp', axis=0, tiled=True)]
    all_to_all x0 -> x1, starting transfers between devices: none -> 18.6 us  [exchange_gather(): shards = lax.all_to_all(shards, name, split_axis=0, concat_axis=0)]
  transfers between devices with their start and end apart: 8 -> 8, of which waited for: 6 -> 5; matrix products, arithmetic and copies ran while one was open for 10% -> 12% of each run, Pallas kernels for 0% -> 0%
where the time goes in v1:
time: 311 us; the launch traced here: 310 us
  waiting for transfers between devices  115 us (37%)
  blocking collectives  82.8 us (27%)
  matrix products  39.5 us (13%)
  starting transfers between devices  33.7 us (11%)
  between operations  14.7 us (5%)
  local copies, waits for them, and re-layouts  14.4 us (5%)
  other arithmetic  9.78 us (3%)
    unnamed x1, blocking collectives  82.8 us
    reduce_scatter x1, waiting for transfers between devices, shards(): lax.psum_scatter(jnp.dot(inner, down_weight, preferred_element_type=jnp.f...  36.9 us
    all_gather x1, waiting for transfers between devices, shards(): gathered = lax.all_gather(normed_mlp, 'mlp', axis=0, tiled=True)  28.8 us
    all_gather x1, waiting for transfers between devices, shards(): lax.all_gather(qkv[:, 2 * width:], 'mlp', axis=0, tiled=True)  26.3 us
    all_to_all x1, starting transfers between devices, exchange_gather(): shards = lax.all_to_all(shards, name, split_axis=0, concat_axis=0)  18.6 us
    all_gather x1, waiting for transfers between devices, shards(): lax.all_gather(qkv[:, width:2 * width], 'mlp', axis=0, tiled=True)  18 us
    all_to_all x1, starting transfers between devices, shards(): lax.all_to_all(local_mod, 'req', split_axis=0, concat_axis=2, tiled=True)[0]  11.6 us
    dot_general x1, matrix products, shards(): jnp.dot(inner, down_weight, preferred_element_type=jnp.float32)  7.81 us
  transfers between devices with their start and end apart: 8, of which 5 were waited for; matrix products, arithmetic and copies ran while one was open for 12% of the time, Pallas kernels for 0%

profile of v1, /device:TPU:8, one launch (start us, length us, event | category | flops | bytes accessed | tf_op | source)
XLA Modules:
  0.0 310.1 jit_solution(1463989959308202274)
XLA Ops:
  6.5 0.7 all-gather.5.cloned.1.call-update
  7.3 0.8 convert_element_type.94
  8.2 0.7 convert_element_type.96
  8.9 0.7 convert_element_type.98
  9.6 0.7 broadcast_select_fusion
  10.4 0.7 convert_element_type.100
  11.4 1.8 convolution_add_fusion.3
  13.2 3.0 fusion.29
  16.9 11.6 %all-to-all-start = ((bf16[16,4,576]{2,1,0:T(4,128)(2,1)}), bf16[16,4,576]{2,1,0:T(4,128)(2,1)S(1)}, u32[]{:S(2)}, u32[]{:S(2)}) async-start(bf16[16,4,576]{2,1,0:T(4,128)(2,1)} %reshape.151), calls=%async_computation | async-start | bytes 163840 | tf_op jit(solution)/shard_map/all_to_all | solution.py:109
  31.1 82.8 %all-reduce.2 = (bf16[3456]{0:T(1024)(128)(2,1)S(1)}, bf16[1152]{0:T(1024)(128)(2,1)S(1)}) all-reduce(bf16[3456]{0:T(1024)(128)(2,1)S(1)} %dynamic-update-slice, bf16[1152]{0:T(1024)(128)(2,1)S(1)} %dynamic-update-slice.1), channel_id=1, replica_groups=mesh['cfg'=2,'req'=16,'mlp'=8] {'req'}, use_global_device_ids=true, to_apply=%add | all-reduce | flops 4608 | bytes 18432
  114.6 3.0 fusion.67
  117.6 6.1 %fusion.2 = bf16[128,3456]{1,0:T(8,128)(2,1)S(1)} fusion(bf16[1152,3456]{0,1:T(8,128)(2,1)} %all-gather.5.cloned.1.call-done, f32[3456]{0:T(1024)S(1)} %convert_element_type.103, bf16[1,128,1152]{2,1,0:T(8,128)(2,1)S(1)} %copy-done.1, f32[128,9216]{1,0:T(8,128)} %fusion.67, f32[128]{0:T(128)S(1)} %add_rsqrt_fusion.2, f32[128]{0:T(128)S(1)} %broadcast_multiply_fusion.2), kind=kOutput, calls=%fused_computation.5 | convolution fusion | flops 1021132800 | bytes 10336768 | tf_op jit(solution)/shard_map/dot_general | solution.py:128
  123.7 0.9 fusion.83
  124.7 0.7 all-gather.7.cloned.1.call-update
  125.4 1.7 stack.2
  127.1 18.6 %all-to-all-start.1 = ((bf16[16,1152,72]{1,2,0:T(8,128)(2,1)}), bf16[16,1152,72]{1,2,0:T(8,128)(2,1)}, u32[]{:S(2)}, u32[]{:S(2)}) async-start(bf16[16,1152,72]{1,2,0:T(8,128)(2,1)} %stack.2), calls=%async_computation.1 | async-start | bytes 5308416 | tf_op jit(solution)/shard_map/all_to_all | solution.py:16
  145.9 0.8 broadcast_compare_fusion
  146.9 18.0 %all-gather.9.cloned.1.call-done = bf16[1024,1152]{1,0:T(8,128)(2,1)} async-done(((bf16[128,1152]{1,0:T(8,128)(2,1)}), bf16[1024,1152]{1,0:T(8,128)(2,1)}) %all-gather.9.cloned.1.call-update) | async-done | bytes 2359312 | tf_op jit(solution)/shard_map/all_gather | solution.py:132
  164.9 4.3 %copy.53 = bf16[1024,1152]{0,1:T(8,128)(2,1)} copy(bf16[1024,1152]{1,0:T(8,128)(2,1)} %all-gather.9.cloned.1.call-done) | data formatting | bytes 4718592 | tf_op jit(solution)/shard_map/all_gather | solution.py:132
  169.2 26.3 %all-gather.7.cloned.1.call-done = bf16[1024,1152]{1,0:T(8,128)(2,1)} async-done(((bf16[128,1152]{1,0:T(8,128)(2,1)}), bf16[1024,1152]{1,0:T(8,128)(2,1)}) %all-gather.7.cloned.1.call-update) | async-done | bytes 2359312 | tf_op jit(solution)/shard_map/all_gather | solution.py:133
  195.5 4.3 %copy.51 = bf16[1024,1152]{0,1:T(8,128)(2,1)} copy(bf16[1024,1152]{1,0:T(8,128)(2,1)} %all-gather.7.cloned.1.call-done) | data formatting | bytes 4718592 | tf_op jit(solution)/shard_map/all_gather | solution.py:133
  199.8 7.5 %fusion.84 = (f32[16,128]{1,0:T(8,128)S(1)}, bf16[16,128,1024]{2,1,0:T(8,128)(2,1)}) fusion(pred[128,1024]{1,0:T(8,128)(4,1)S(1)} %copy-done.3, bf16[128,16,72]{0,2,1:T(8,128)(2,1)S(1)} %bitcast.91, bf16[1024,16,72]{0,2,1:T(8,128)(2,1)} %bitcast.87), kind=kOutput, calls=%fused_computation.112 | convolution fusion | flops 314573824 | bytes 6987776 | tf_op jit(solution)/shard_map/sub | solution.py:46
  207.2 5.2 %fusion.26 = bf16[128,16,72]{0,2,1:T(8,128)(2,1)} fusion(bf16[1024,16,72]{0,2,1:T(8,128)(2,1)} %bitcast.88, bf16[16,128,1024]{2,1,0:T(8,128)(2,1)} %get-tuple-element.18, f32[128,16]{0,1:T(8,128)S(1)} %bitcast.98), kind=kOutput, calls=%fused_computation.31 | convolution fusion | flops 302284800 | bytes 6856704 | tf_op jit(solution)/shard_map/hqk,khd->qhd/dot_general | solution.py:49
  212.4 3.0 fusion.85
  215.7 2.2 fusion.41
  217.9 28.8 %all-gather.11.cloned.1.call-done = bf16[1024,1152]{1,0:T(8,128)(2,1)} async-done(((bf16[128,1152]{1,0:T(8,128)(2,1)}), bf16[1024,1152]{1,0:T(8,128)(2,1)}) %all-gather.11.cloned.1.call-update) | async-done | bytes 2359312 | tf_op jit(solution)/shard_map/all_gather | solution.py:147
  246.7 7.8 %convolution_convert_fusion = bf16[1024,1152]{1,0:T(8,128)(2,1)} fusion(bf16[576,1152]{1,0:T(8,128)(2,1)} %param.46, bf16[1024,1152]{1,0:T(8,128)(2,1)} %all-gather.11.cloned.1.call-done, bf16[1152,576]{0,1:T(8,128)(2,1)} %param.44, f32[576]{0:T(1024)S(1)} %convert_element_type.111), kind=kOutput, calls=%fused_computation.11 | convolution fusion | flops 2724986880 | bytes 7375104 | tf_op jit(solution)/shard_map/dot_general | solution.py:154
  255.2 36.9 %reduce-scatter.2.cloned.1.call-done = bf16[128,1152]{1,0:T(8,128)(2,1)} async-done(((bf16[1024,1152]{1,0:T(8,128)(2,1)}), bf16[128,1152]{1,0:T(8,128)(2,1)}) %reduce-scatter.2.cloned.1.call-update) | async-done | bytes 294928 | tf_op jit(solution)/shard_map/reduce_scatter | solution.py:153
  292.2 1.3 fusion.81
  293.7 2.2 convolution_add_fusion.6
  295.9 3.2 %all-to-all-start.2 = ((f32[1,128,16]{1,0,2:T(1,128)}), f32[1,128,16]{1,0,2:T(1,128)S(1)}, u32[]{:S(2)}, u32[]{:S(2)}) async-start(f32[1,128,16]{1,0,2:T(1,128)} %bitcast.18), calls=%async_computation.3 | async-start | bytes 16384 | tf_op jit(solution)/shard_map/all_to_all | solution.py:168
  299.2 3.7 %all-to-all-done.2 = f32[1,128,16]{1,0,2:T(1,128)S(1)} async-done(((f32[1,128,16]{1,0,2:T(1,128)}), f32[1,128,16]{1,0,2:T(1,128)S(1)}, u32[]{:S(2)}, u32[]{:S(2)}) %all-to-all-start.2) | async-done | bytes 8224 | tf_op jit(solution)/shard_map/all_to_all | solution.py:168
  (78 shorter events, 5.6 us)
Async XLA Ops:
  6.5 4.8 %copy-start = (bf16[1152,1152]{1,0:T(8,128)(2,1)S(1)}, bf16[1152,1152]{1,0:T(8,128)(2,1)}, u32[]{:S(2)}) copy-start(bf16[1152,1152]{1,0:T(8,128)(2,1)} %param.36) | copy-start | bytes 7962628
  6.5 111.0 %all-gather.5.cloned.1.call-start = ((), (), s32[]{:S(2)}) async-start(), calls=%async_computation.4 | async-start | bytes 8460288 | tf_op jit(solution)/shard_map/all_gather | solution.py:122
  13.2 15.4 %copy-start.11 = (s32[1,4]{1,0:T(1,128)S(1)}, s32[1,4]{1,0:T(1,128)}, u32[]{:S(2)}) copy-start(s32[1,4]{1,0:T(1,128)} %param.29) | copy-start | bytes 52
  13.2 15.5 %copy-start.15 = (u32[256]{0:T(256)S(1)}, u32[256]{0:T(256)}, u32[]{:S(2)}) copy-start(u32[256]{0:T(256)} %constant.70) | copy-start | bytes 3076
  13.2 17.4 %copy-start.12 = (bf16[216]{0:T(256)(128)(2,1)S(1)}, bf16[216]{0:T(256)(128)(2,1)}, u32[]{:S(2)}) copy-start(bf16[216]{0:T(256)(128)(2,1)} %param.41) | copy-start | bytes 1300
  13.2 17.7 %copy-start.13 = (bf16[72]{0:T(256)(128)(2,1)S(1)}, bf16[72]{0:T(256)(128)(2,1)}, u32[]{:S(2)}) copy-start(bf16[72]{0:T(256)(128)(2,1)} %param.43) | copy-start | bytes 436
  13.2 100.9 %copy-start.1 = (bf16[1,128,1152]{2,1,0:T(8,128)(2,1)S(1)}, bf16[1,128,1152]{2,1,0:T(8,128)(2,1)}, u32[]{:S(2)}) copy-start(bf16[1,128,1152]{2,1,0:T(8,128)(2,1)} %param.25) | copy-start | bytes 884740
  16.9 97.5 %all-to-all-start = ((bf16[16,4,576]{2,1,0:T(4,128)(2,1)}), bf16[16,4,576]{2,1,0:T(4,128)(2,1)S(1)}, u32[]{:S(2)}, u32[]{:S(2)}) async-start(bf16[16,4,576]{2,1,0:T(4,128)(2,1)} %reshape.151), calls=%async_computation | async-start | bytes 163840 | tf_op jit(solution)/shard_map/all_to_all | solution.py:109
  28.5 136.4 %all-gather.9.cloned.1.call-start = ((), (), s32[]{:S(2)}) async-start(), calls=%async_computation.6 | async-start | bytes 2654208 | tf_op jit(solution)/shard_map/all_gather | solution.py:132
  123.7 1.7 copy-start.2
  124.6 70.8 %all-gather.7.cloned.1.call-start = ((), (), s32[]{:S(2)}) async-start(), calls=%async_computation.5 | async-start | bytes 2654208 | tf_op jit(solution)/shard_map/all_gather | solution.py:133
  127.1 85.3 %all-to-all-start.1 = ((bf16[16,1152,72]{1,2,0:T(8,128)(2,1)}), bf16[16,1152,72]{1,2,0:T(8,128)(2,1)}, u32[]{:S(2)}, u32[]{:S(2)}) async-start(bf16[16,1152,72]{1,2,0:T(8,128)(2,1)} %stack.2), calls=%async_computation.1 | async-start | bytes 5308416 | tf_op jit(solution)/shard_map/all_to_all | solution.py:16
  145.7 101.0 %all-gather.11.cloned.1.call-start = ((), (), s32[]{:S(2)}) async-start(), calls=%async_computation.7 | async-start | bytes 2654208 | tf_op jit(solution)/shard_map/all_gather | solution.py:147
  169.2 30.6 %copy-start.3 = (pred[128,1024]{1,0:T(8,128)(4,1)S(1)}, pred[128,1024]{1,0:T(8,128)(4,1)}, u32[]{:S(2)}) copy-start(pred[128,1024]{1,0:T(8,128)(4,1)} %broadcast_compare_fusion) | copy-start | bytes 393220
  215.4 2.5 copy-start.7
  217.8 74.3 %reduce-scatter.2.cloned.1.call-start = ((), (), s32[]{:S(2)}) async-start(), calls=%async_computation.8 | async-start | bytes 2654208 | tf_op jit(solution)/shard_map/reduce_scatter | solution.py:153
  254.5 0.7 copy-start.5
  254.5 0.7 copy-start.14
  254.5 39.2 %copy-start.4 = (bf16[1152,16]{0,1:T(8,128)(2,1)S(1)}, bf16[1152,16]{0,1:T(8,128)(2,1)}, u32[]{:S(2)}) copy-start(bf16[1152,16]{0,1:T(8,128)(2,1)} %param.48) | copy-start | bytes 110596
  255.2 43.9 %copy-start.8 = (f32[1,4]{1,0:T(1,128)S(1)}, f32[1,4]{1,0:T(1,128)}, u32[]{:S(2)}) copy-start(f32[1,4]{1,0:T(1,128)} %param.31) | copy-start | bytes 52
  255.2 44.0 %copy-start.9 = (f32[1,4]{1,0:T(1,128)S(1)}, f32[1,4]{1,0:T(1,128)}, u32[]{:S(2)}) copy-start(f32[1,4]{1,0:T(1,128)} %param.30) | copy-start | bytes 52
  255.2 44.0 %copy-start.10 = (f32[1,4]{1,0:T(1,128)S(1)}, f32[1,4]{1,0:T(1,128)}, u32[]{:S(2)}) copy-start(f32[1,4]{1,0:T(1,128)} %param.32) | copy-start | bytes 52
  255.2 47.7 %copy-start.6 = (f32[128,8]{0,1:T(8,128)S(1)}, f32[128,8]{0,1:T(8,128)}, u32[]{:S(2)}) copy-start(f32[128,8]{0,1:T(8,128)} %param.26) | copy-start | bytes 12292
  295.9 7.0 %all-to-all-start.2 = ((f32[1,128,16]{1,0,2:T(1,128)}), f32[1,128,16]{1,0,2:T(1,128)S(1)}, u32[]{:S(2)}, u32[]{:S(2)}) async-start(f32[1,128,16]{1,0,2:T(1,128)} %bitcast.18), calls=%async_computation.3 | async-start | bytes 16384 | tf_op jit(solution)/shard_map/all_to_all | solution.py:168
Sparse Core Ops, SparseCore 0:
  9.8 107.0 all-gather.4
  124.8 40.0 all-gather.8
  166.7 28.6 all-gather.6
  218.0 28.6 all-gather.10
  254.6 37.4 reduce-scatter.1
